TPU v7x, 256 devices: a whole 4x4x8 slice. The times are simulated.
256 devices in a mesh: member: 8 (over z_hi, core), tile: 32 (over y, x, z_lo).
Axes of the slice: x: 4, y: 4, z: 8 (z_hi: 4, z_lo: 2; z = z_hi * 2 + z_lo), core: 2. Of those that a mesh axis runs over, the one named last changes fastest.
Arguments:
- upsampled_coarse: bfloat16 [128, 32, 256], P('tile'), may hold values from -6 to 6
- target: bfloat16 [128, 32, 256], P('tile'), may hold values from -6 to 6
- seeds: int32 [16], P('member'), may hold values from 0 to 63
- band_row: int32 [1], replicated, may hold values from 0 to 1920
- noise_bank: float32 [64, 16], replicated, may hold values from -5 to 5
- cond_weight: float32 [16, 256], replicated, may hold values from -1.5 to 1.5
- conv_in: bfloat16 [3, 3, 32, 128], replicated, may hold values from -0.375 to 0.375
- conv_mid: bfloat16 [3, 3, 128, 128], replicated, may hold values from -0.1875 to 0.1875
- conv_out: bfloat16 [3, 3, 128, 128], replicated, may hold values from -0.1875 to 0.1875
- head_weight: bfloat16 [128, 32], replicated, may hold values from -0.5 to 0.5
- per_quantity_offset: float32 [32], replicated, may hold values from -3 to 3
Outputs:
- crps_map: float32 [128, 32, 256], P('tile', 'member')
- conv_grad: float32 [3, 3, 128, 128], replicated
- head_grad: float32 [128, 32], replicated
- bias_grad: float32 [32], replicated
Inputs may be any that keep to these rules, and one draw needn't show every extreme that they name: `band_row`: the band lies inside the grid.
All inputs are finite; a program needn't handle non-finite values.
Results may differ from a plain program's by a relative error of at most 0.0015.
Values may be sent and summed in bfloat16 or wider, within the bound.
No kernel may reach another device: no remote copies, remote signals or barrier semaphores. Data moves between devices by JAX's collectives and lax.ppermute only.
A program may use at most 64 MiB of HBM per device.

v0:
```python
import math
import jax
import jax.numpy as jnp
from jax import lax
from jax.sharding import Mesh, PartitionSpec as P

GRID_ROWS = 2048
MEMBER = ("group", "core")


def extended(x, sides, width):
    for axis, dim in sides:
        devices, length = (lax.axis_size(axis), x.shape[dim])
        up = [(i, (i + 1) % devices) for i in range(devices - 1)]
        down = [(j, i) for i, j in up]
        before = lax.slice_in_dim(lax.ppermute(x, axis, up), length - width, length, axis=dim)
        after = lax.slice_in_dim(lax.ppermute(x, axis, down), 0, width, axis=dim)
        x = jnp.concatenate([before, x, after], axis=dim)
    return x


def input_conv(padded, kernel):
    out_rows = padded.shape[0] - 2
    col_count = padded.shape[2]
    wide = jnp.pad(padded, ((0, 0), (0, 0), (1, 1)))
    shifted = jnp.concatenate(
        [wide[i : i + out_rows, :, j : j + col_count] for i in range(3) for j in range(3)], axis=1
    )
    return jnp.einsum(
        "rkw,kc->rwc",
        shifted,
        kernel.reshape(-1, kernel.shape[3]),
        preferred_element_type=jnp.float32,
    )


def feature_conv(padded, kernel):
    out_rows = padded.shape[1] - 2
    col_count = padded.shape[2]
    wide = jnp.pad(padded, ((0, 0), (0, 0), (1, 1), (0, 0)))
    shifted = jnp.concatenate([wide[:, :, j : j + col_count] for j in range(3)], axis=3)
    summed = jnp.zeros((padded.shape[0], out_rows, col_count, kernel.shape[3]), jnp.float32)
    for i in range(3):
        summed = summed + jnp.einsum(
            "mrwc,cd->mrwd",
            shifted[:, i : i + out_rows],
            kernel[i].reshape(-1, kernel.shape[3]),
            preferred_element_type=jnp.float32,
        )
    return summed


def condition(base, cond_scale, cond_shift):
    average = jnp.mean(base, axis=-1, keepdims=True)
    centred = base - average
    spread = jnp.mean(centred * centred, axis=-1, keepdims=True)
    normed = centred * lax.rsqrt(spread + 1e-05)
    mixed = normed[None] * (1.0 + cond_scale[:, None, None, :]) + cond_shift[:, None, None, :]
    return jax.nn.gelu(mixed).astype(jnp.bfloat16)


def abs_terms(probe, sample_group_predictions):

    def abs_single(member_index):
        return jnp.sum(jnp.abs(member_index[None] - sample_group_predictions), axis=0)

    return lax.map(abs_single, probe)


def sign_terms(probe, sample_group_predictions):

    def sign_single(member_index):
        return jnp.sum(jnp.sign(member_index[None] - sample_group_predictions), axis=0)

    return lax.map(sign_single, probe)


def all_reduce_sum(parts):
    peers = ("group", "tile")
    devices = lax.axis_size("group") * lax.axis_size("tile")
    flat = jnp.concatenate([p.reshape(-1) for p in parts])
    total = flat.shape[0]
    width = -(-total // (2 * devices * 128)) * 128
    flat = jnp.pad(flat, (0, 2 * width * devices - total)).reshape(2, devices * width)
    core = lax.axis_index("core")
    swap = [(0, 1), (1, 0)]
    first = core == 0
    keep = jnp.where(first, flat[0], flat[1])
    half = keep + lax.ppermute(jnp.where(first, flat[1], flat[0]), "core", swap)
    pieces = lax.all_to_all(half.reshape(devices, width), peers, 0, 0, tiled=True)
    own = jnp.sum(pieces, axis=0, keepdims=True)
    summed = lax.all_to_all(jnp.broadcast_to(own, (devices, width)), peers, 0, 0, tiled=True)
    summed = summed.reshape(-1)
    other = lax.ppermute(summed, "core", swap)
    spread = jnp.where(first, jnp.concatenate([summed, other]), jnp.concatenate([other, summed]))
    out, at = ([], 0)
    for p in parts:
        out.append(spread[at : at + p.size].reshape(p.shape))
        at += p.size
    return tuple(out)


def on_device(
    upsampled_coarse,
    target,
    seeds,
    band_row,
    noise_bank,
    cond_weight,
    conv_in,
    conv_mid,
    conv_out,
    head_weight,
    per_quantity_offset,
):
    channels = conv_mid.shape[3]
    row_count = upsampled_coarse.shape[0]
    var_count = upsampled_coarse.shape[1]
    col_count = upsampled_coarse.shape[2]
    tile_count = lax.axis_size("tile")
    tile_at = lax.axis_index("tile")
    band_rows = row_count * tile_count
    selector = (seeds[:, None] == jnp.arange(noise_bank.shape[0], dtype=jnp.int32)[None]).astype(
        jnp.float32
    )
    noise_vec = jnp.dot(selector, noise_bank, precision=lax.Precision.HIGHEST)
    random_latent_gain = jnp.dot(noise_vec, cond_weight, precision=lax.Precision.HIGHEST)
    cond_scale = random_latent_gain[:, :channels]
    cond_shift = random_latent_gain[:, channels:]
    input_padded = extended(upsampled_coarse, (("tile", 0),), 3)
    band_at = tile_at * row_count + jnp.arange(-2, row_count + 2, dtype=jnp.int32)
    inside = ((band_at >= 0) & (band_at < band_rows))[None, :, None, None]
    first_wide = condition(input_conv(input_padded, conv_in), cond_scale, cond_shift)
    first_wide = jnp.where(inside, first_wide, jnp.zeros_like(first_wide))
    first_hidden = first_wide[:, 2 : 2 + row_count]
    second_padded = jax.nn.gelu(feature_conv(first_wide, conv_mid)).astype(jnp.bfloat16)
    second_padded = jnp.where(inside[:, 1:-1], second_padded, jnp.zeros_like(second_padded))
    final_linear_response = feature_conv(second_padded, conv_out)
    latent_layer_three = (
        first_hidden.astype(jnp.float32) + jax.nn.gelu(final_linear_response)
    ).astype(jnp.bfloat16)
    final_layer_result = jnp.einsum(
        "mrwc,cv->vmrw", latent_layer_three, head_weight, preferred_element_type=jnp.float32
    )
    sample_prediction = (
        final_layer_result
        + jnp.transpose(upsampled_coarse, (1, 0, 2)).astype(jnp.float32)[:, None]
        + per_quantity_offset[:, None, None, None]
    ).astype(jnp.bfloat16)
    row_global = band_row[0] + tile_at * row_count + jnp.arange(row_count, dtype=jnp.int32)
    latitude = math.pi * (row_global.astype(jnp.float32) + 0.5) / GRID_ROWS - math.pi / 2
    row_factor = (jnp.cos(latitude) / (band_rows * col_count))[None, None, :, None]
    var_share = var_count // (lax.axis_size("group") * lax.axis_size("core"))
    var_start = lax.axis_index(MEMBER) * var_share
    collected_members = lax.all_to_all(
        sample_prediction, MEMBER, split_axis=0, concat_axis=1, tiled=True
    )
    sample_group_predictions = collected_members.astype(jnp.float32)
    member_count = sample_group_predictions.shape[1]
    truth = jnp.transpose(
        lax.dynamic_slice_in_dim(target, var_start, var_share, 1), (1, 0, 2)
    ).astype(jnp.float32)[:, None]
    pair_differ = sample_group_predictions[:, :, None] - sample_group_predictions[:, None, :]
    abs_sums = jnp.sum(jnp.abs(pair_differ), axis=2)
    sign_sums = jnp.sum(jnp.sign(pair_differ), axis=2)
    crps_share = jnp.mean(jnp.abs(sample_group_predictions - truth), axis=1) - jnp.sum(
        abs_sums, axis=1
    ) / (2 * member_count * (member_count - 1))
    crps_map = jnp.transpose(crps_share, (1, 0, 2))
    cot_share = (
        row_factor
        * (
            jnp.sign(sample_group_predictions - truth) / member_count
            - sign_sums / (member_count * (member_count - 1))
        )
    ).astype(jnp.bfloat16)
    cotangent = lax.all_to_all(cot_share, MEMBER, split_axis=1, concat_axis=0, tiled=True)
    head_grad = jnp.einsum(
        "mrwc,vmrw->cv", latent_layer_three, cotangent, preferred_element_type=jnp.float32
    )
    bias_grad = jnp.sum(cotangent.astype(jnp.float32), axis=(1, 2, 3))
    back = jnp.einsum("vmrw,cv->mrwc", cotangent, head_weight, preferred_element_type=jnp.float32)
    unused_out, pullback = jax.vjp(jax.nn.gelu, final_linear_response)
    slope = lax.optimization_barrier(pullback(jnp.ones_like(final_linear_response))[0])
    d_pre = (back * slope).astype(jnp.bfloat16)
    second_wide = jnp.pad(second_padded, ((0, 0), (0, 0), (1, 1), (0, 0)))
    rows_of = []
    for i in range(3):
        cols_of = []
        for j in range(3):
            cols_of.append(
                jnp.einsum(
                    "mrwc,mrwd->cd",
                    second_wide[:, i : i + row_count, j : j + col_count],
                    d_pre,
                    preferred_element_type=jnp.float32,
                )
            )
        rows_of.append(jnp.stack(cols_of))
    conv_grad = jnp.stack(rows_of)
    conv_grad, head_grad_t, bias_grad = all_reduce_sum((conv_grad, head_grad.T, bias_grad))
    head_grad = head_grad_t.T
    return (crps_map, conv_grad, head_grad, bias_grad)


def solution(mesh):
    members = mesh.shape["member"]
    split = Mesh(
        mesh.devices.reshape(members // 2, 2, mesh.shape["tile"]), ("group", "core", "tile")
    )
    return jax.shard_map(
        on_device,
        mesh=split,
        in_specs=(
            P("tile", None, None),
            P("tile", None, None),
            P(MEMBER),
            P(),
            P(),
            P(),
            P(),
            P(),
            P(),
            P(),
            P(),
        ),
        out_specs=(P("tile", MEMBER, None), P(), P(), P()),
        check_vma=False,
    )
```

profile of v0, /device:TPU:1, one launch (start us, length us, event | category | flops | bytes accessed | tf_op | source)
XLA Modules:
  0.0 115.7 jit_solution(1448701602072918489)
XLA Ops:
  0.7 4.5 %collective-permute-start = (bf16[4,32,256]{2,1,0:T(8,128)(2,1)}, bf16[4,32,256]{2,1,0:T(8,128)(2,1)S(1)}, u32[]{:S(2)}, u32[]{:S(2)}) collective-permute-start(bf16[4,32,256]{2,1,0:T(8,128)(2,1)} %param.11), channel_id=1, source_target_pairs={{0,1},{1,2},{2,3},{3,4},{4,5},{5,6},{6,7},{7,8},{8,9},{9,10},{10,1... | collective-permute-start | bytes 196616 | tf_op jit(solution)/shard_map/ppermute | solution.py:16
  5.2 1.3 %collective-permute-start.1 = (bf16[4,32,256]{2,1,0:T(8,128)(2,1)}, bf16[4,32,256]{2,1,0:T(8,128)(2,1)S(1)}, u32[]{:S(2)}, u32[]{:S(2)}) collective-permute-start(bf16[4,32,256]{2,1,0:T(8,128)(2,1)} %param.11), channel_id=1, source_target_pairs={{1,0},{2,1},{3,2},{4,3},{5,4},{6,5},{7,6},{8,7},{9,8},{10,9},{11,1... | collective-permute-start | bytes 196616 | tf_op jit(solution)/shard_map/ppermute | solution.py:17
  6.5 0.9 convert_bitcast_fusion
  7.3 0.9 fusion.54
  8.2 0.8 fusion.70
  9.1 1.0 fusion.68
  10.2 1.0 fusion.67
  12.0 0.5 fusion.69
  12.8 0.3 copy.96
  13.1 0.9 fusion.23
  14.0 0.6 pad_slice_fusion.1
  14.6 0.8 fusion.65
  15.4 0.8 fusion.66
  16.2 1.2 %fusion.22 = bf16[2,6,256,128]{3,2,1,0:T(8,128)(2,1)S(1)} fusion(bf16[384,128,1,1]{1,0,3,2:T(8,128)(2,1)S(1)} %bitcast.189, f32[2,6,256,128]{3,2,1,0:T(8,128)S(1)} %fusion.66, f32[2,6,256,128]{3,2,1,0:T(8,128)S(1)} %fusion.65, pred[6]{0:T(512)(128)(4,1)S(1)} %slice_bitcast_fusion, bf16[2,8,256,128]{3,2,1,0:T(8,128)(2,1)S(1)} %get-tuple-element.21, ...), kind=kOutput, calls=%fused_computation.44 | convolution fusion | flops 316145664 | bytes 7176198 | tf_op jit(solution)/shard_map/mrwc,cd->mrwd/dot_general | solution.py:44
  17.4 0.4 pad_slice_fusion.9
  17.8 0.6 fusion.64
  18.4 0.6 convolution_add_fusion.1
  19.0 1.4 %fusion.29 = (f32[2,4,256,128]{3,2,1,0:T(8,128)S(1)}, bf16[2,4,256,128]{3,2,1,0:T(8,128)(2,1)S(1)}) fusion(bf16[2,8,256,128]{3,2,1,0:T(8,128)(2,1)S(1)} %fusion.23, f32[2,4,256,128]{3,2,1,0:T(8,128)S(1)} %convolution_add_fusion.1, bf16[384,128,1,1]{1,0,3,2:T(8,128)(2,1)S(1)} %bitcast.186, bf16[2,6,256,128]{3,2,1,0:T(8,128)(2,1)S(1)} %get-tuple-element.23, ...), kind=kOutput, calls=%fused_computation.51 | convolution fusion | flops 214171648 | bytes 5603328 | tf_op jit(solution)/shard_map/mrwc,cd->mrwd/dot_general | solution.py:44
  20.4 0.3 fusion.21
  20.7 0.8 copy.97
  21.5 8.8 %all-to-all-start = ((bf16[32,2,4,256]{3,2,1,0:T(4,128)(2,1)}), bf16[32,2,4,256]{3,2,1,0:T(4,128)(2,1)S(1)}, u32[]{:S(2)}, u32[]{:S(2)}) async-start(bf16[32,2,4,256]{3,2,1,0:T(4,128)(2,1)} %copy.97), calls=%async_computation | async-start | bytes 262144 | tf_op jit(solution)/shard_map/all_to_all | solution.py:155
  30.2 0.7 convert_bitcast_fusion.1
  31.6 6.9 %all-to-all-done = bf16[32,2,4,256]{3,2,1,0:T(4,128)(2,1)S(1)} async-done(((bf16[32,2,4,256]{3,2,1,0:T(4,128)(2,1)}), bf16[32,2,4,256]{3,2,1,0:T(4,128)(2,1)S(1)}, u32[]{:S(2)}, u32[]{:S(2)}) %all-to-all-start) | async-done | bytes 131104 | tf_op jit(solution)/shard_map/all_to_all | solution.py:155
  38.6 2.3 %fusion.1 = (f32[4,16,4,256]{3,2,1,0:T(4,128)S(1)}, f32[4,4,256]{2,1,0:T(4,128)S(1)}) fusion(f32[4,16,4,256]{3,1,2,0:T(8,128)S(1)} %copy.100, f32[4,16,4,256]{3,2,1,0:T(4,128)S(1)} %bitcast.175), kind=kLoop, calls=%fused_computation.3 | loop fusion | flops 5173248 | bytes 802816 | tf_op jit(solution)/shard_map/reduce_sum | solution.py:165
  41.2 0.7 copy.102
  41.9 4.3 %all-to-all-start.1 = ((bf16[4,16,4,256]{3,2,0,1:T(4,128)(2,1)}), bf16[4,16,4,256]{3,2,0,1:T(4,128)(2,1)S(1)}, u32[]{:S(2)}, u32[]{:S(2)}) async-start(bf16[4,16,4,256]{3,2,0,1:T(4,128)(2,1)} %copy.102), calls=%async_computation.1 | async-start | bytes 262144 | tf_op jit(solution)/shard_map/all_to_all | solution.py:177
  46.2 8.7 %all-to-all-done.1 = bf16[4,16,4,256]{3,2,0,1:T(4,128)(2,1)S(1)} async-done(((bf16[4,16,4,256]{3,2,0,1:T(4,128)(2,1)}), bf16[4,16,4,256]{3,2,0,1:T(4,128)(2,1)S(1)}, u32[]{:S(2)}, u32[]{:S(2)}) %all-to-all-start.1) | async-done | bytes 131104 | tf_op jit(solution)/shard_map/all_to_all | solution.py:177
  55.2 0.4 fusion.18
  55.6 0.3 convolution_bitcast_fusion.7
  55.9 0.3 convolution_bitcast_fusion.2
  56.3 0.3 convolution_bitcast_fusion.6
  56.6 0.3 convolution_bitcast_fusion.9
  57.0 0.3 convolution_bitcast_fusion.3
  57.3 0.3 convolution_bitcast_fusion.8
  57.7 0.3 convolution_bitcast_fusion.5
  58.0 0.3 convolution_bitcast_fusion.1
  58.4 0.3 convolution_bitcast_fusion.4
  59.3 1.3 %collective-permute-start.2 = (f32[81920]{0:T(1024)S(1)}, f32[81920]{0:T(1024)S(1)}, u32[]{:S(2)}, u32[]{:S(2)}) collective-permute-start(f32[81920]{0:T(1024)S(1)} %slice_select_fusion), channel_id=1, source_target_pairs={{0,32},{32,0},{1,33},{33,1},{2,34},{34,2},{3,35},{35,3},{4,36},{36... | collective-permute-start | bytes 983048 | tf_op jit(solution)/shard_map/ppermute | solution.py:89
  60.6 1.3 %collective-permute-done.2 = f32[81920]{0:T(1024)S(1)} collective-permute-done((f32[81920]{0:T(1024)S(1)}, f32[81920]{0:T(1024)S(1)}, u32[]{:S(2)}, u32[]{:S(2)}) %collective-permute-start.2) | collective-permute-done | bytes 327712 | tf_op jit(solution)/shard_map/ppermute | solution.py:89
  61.9 27.0 %all_to_all.42 = f32[128,1,640]{2,1,0:T(1,128)S(1)} all-to-all(f32[128,1,640]{2,1,0:T(1,128)S(1)} %bitcast.181), channel_id=1, replica_groups=mesh['group'=4,'core'=2,'tile'=32] {'group','tile'}, dimensions={0} | all-to-all | bytes 655360 | tf_op jit(solution)/shard_map/all_to_all | solution.py:90
  88.9 0.2 reduce_sum.76
  89.3 19.7 %all_to_all.43 = f32[128,1,640]{2,1,0:T(1,128)S(1)} all-to-all(f32[128,1,640]{2,1,0:T(1,128)S(1)} %broadcast_in_dim.29), channel_id=1, replica_groups=mesh['group'=4,'core'=2,'tile'=32] {'group','tile'}, dimensions={0} | all-to-all | bytes 655360 | tf_op jit(solution)/shard_map/all_to_all | solution.py:92
  109.0 3.4 %collective-permute-start.3 = (f32[81920]{0:T(1024)S(1)}, f32[81920]{0:T(1024)S(1)}, u32[]{:S(2)}, u32[]{:S(2)}) collective-permute-start(f32[81920]{0:T(1024)S(1)} %bitcast.177), channel_id=1, source_target_pairs={{0,32},{32,0},{1,33},{33,1},{2,34},{34,2},{3,35},{35,3},{4,36},{36... | collective-permute-start | bytes 983048 | tf_op jit(solution)/shard_map/ppermute | solution.py:94
  112.5 0.6 copy.116
  113.1 0.5 collective-permute-done.3
  113.7 0.9 slice.204
  114.6 0.5 slice.205
  115.1 0.6 fusion.51
  (52 shorter events, 2.6 us)
Async XLA Ops:
  0.6 11.4 %copy-start = (bf16[3,3,32,128]{3,2,1,0:T(8,128)(2,1)S(1)}, bf16[3,3,32,128]{3,2,1,0:T(8,128)(2,1)}, u32[]{:S(2)}) copy-start(bf16[3,3,32,128]{3,2,1,0:T(8,128)(2,1)} %param.17) | copy-start | bytes 221188
  0.6 10.6 %copy-start.1 = (bf16[4,32,256]{2,1,0:T(8,128)(2,1)S(1)}, bf16[4,32,256]{2,1,0:T(8,128)(2,1)}, u32[]{:S(2)}) copy-start(bf16[4,32,256]{2,1,0:T(8,128)(2,1)} %param.11) | copy-start | bytes 196612
  0.7 10.6 %collective-permute-start = (bf16[4,32,256]{2,1,0:T(8,128)(2,1)}, bf16[4,32,256]{2,1,0:T(8,128)(2,1)S(1)}, u32[]{:S(2)}, u32[]{:S(2)}) collective-permute-start(bf16[4,32,256]{2,1,0:T(8,128)(2,1)} %param.11), channel_id=1, source_target_pairs={{0,1},{1,2},{2,3},{3,4},{4,5},{5,6},{6,7},{7,8},{8,9},{9,10},{10,1... | collective-permute-start | bytes 196616 | tf_op jit(solution)/shard_map/ppermute | solution.py:16
  5.2 6.1 %collective-permute-start.1 = (bf16[4,32,256]{2,1,0:T(8,128)(2,1)}, bf16[4,32,256]{2,1,0:T(8,128)(2,1)S(1)}, u32[]{:S(2)}, u32[]{:S(2)}) collective-permute-start(bf16[4,32,256]{2,1,0:T(8,128)(2,1)} %param.11), channel_id=1, source_target_pairs={{1,0},{2,1},{3,2},{4,3},{5,4},{6,5},{7,6},{8,7},{9,8},{10,9},{11,1... | collective-permute-start | bytes 196616 | tf_op jit(solution)/shard_map/ppermute | solution.py:17
  19.0 1.4 %copy-start.2 = (bf16[128,32]{0,1:T(8,128)(2,1)S(1)}, bf16[128,32]{0,1:T(8,128)(2,1)}, u32[]{:S(2)}) copy-start(bf16[128,32]{0,1:T(8,128)(2,1)} %param.20) | copy-start | bytes 24580
  19.0 1.4 %copy-start.3 = (f32[32]{0:T(128)S(1)}, f32[32]{0:T(128)}, u32[]{:S(2)}) copy-start(f32[32]{0:T(128)} %param.21) | copy-start | bytes 388
  21.5 17.1 %all-to-all-start = ((bf16[32,2,4,256]{3,2,1,0:T(4,128)(2,1)}), bf16[32,2,4,256]{3,2,1,0:T(4,128)(2,1)S(1)}, u32[]{:S(2)}, u32[]{:S(2)}) async-start(bf16[32,2,4,256]{3,2,1,0:T(4,128)(2,1)} %copy.97), calls=%async_computation | async-start | bytes 262144 | tf_op jit(solution)/shard_map/all_to_all | solution.py:155
  41.9 13.1 %all-to-all-start.1 = ((bf16[4,16,4,256]{3,2,0,1:T(4,128)(2,1)}), bf16[4,16,4,256]{3,2,0,1:T(4,128)(2,1)S(1)}, u32[]{:S(2)}, u32[]{:S(2)}) async-start(bf16[4,16,4,256]{3,2,0,1:T(4,128)(2,1)} %copy.102), calls=%async_computation.1 | async-start | bytes 262144 | tf_op jit(solution)/shard_map/all_to_all | solution.py:177
  59.3 2.6 %collective-permute-start.2 = (f32[81920]{0:T(1024)S(1)}, f32[81920]{0:T(1024)S(1)}, u32[]{:S(2)}, u32[]{:S(2)}) collective-permute-start(f32[81920]{0:T(1024)S(1)} %slice_select_fusion), channel_id=1, source_target_pairs={{0,32},{32,0},{1,33},{33,1},{2,34},{34,2},{3,35},{35,3},{4,36},{36... | collective-permute-start | bytes 983048 | tf_op jit(solution)/shard_map/ppermute | solution.py:89
  109.0 4.6 %collective-permute-start.3 = (f32[81920]{0:T(1024)S(1)}, f32[81920]{0:T(1024)S(1)}, u32[]{:S(2)}, u32[]{:S(2)}) collective-permute-start(f32[81920]{0:T(1024)S(1)} %bitcast.177), channel_id=1, source_target_pairs={{0,32},{32,0},{1,33},{33,1},{2,34},{34,2},{3,35},{35,3},{4,36},{36... | collective-permute-start | bytes 983048 | tf_op jit(solution)/shard_map/ppermute | solution.py:94
where the time goes:
time: 116 us
  blocking collectives  46.7 us (40%)
  starting transfers between devices  23.6 us (20%)
  waiting for transfers between devices  17.4 us (15%)
  matrix products  11.4 us (10%)
  local copies, waits for them, and re-layouts  8.12 us (7%)
  other arithmetic  6.7 us (6%)
  between operations  1.76 us (2%)
    all_to_all x1, blocking collectives, all_reduce_sum(): lax.all_to_all(half.reshape(devices, width), peers, 0, 0, tiled=True)  27 us
    all_to_all x1, blocking collectives, all_reduce_sum(): lax.all_to_all(jnp.broadcast_to(own, (devices, width)), peers, 0, 0, tile...  19.7 us
    all_to_all x1, starting transfers between devices, on_device(): lax.all_to_all(sample_prediction, MEMBER, split_axis=0, concat_axis=1, ti...  8.75 us
    all_to_all x1, waiting for transfers between devices, on_device(): lax.all_to_all(cot_share, MEMBER, split_axis=1, concat_axis=0, tiled=True)  8.71 us
    all_to_all x1, waiting for transfers between devices, on_device(): lax.all_to_all(sample_prediction, MEMBER, split_axis=0, concat_axis=1, ti...  6.9 us
    dot_general x6, matrix products, feature_conv(): jnp.einsum('mrwc,cd->mrwd', shifted[:, i:i + out_rows], kernel[i].reshape...  5.26 us
    ppermute x1, starting transfers between devices, extended(): lax.ppermute(x, axis, up)  4.49 us
    all_to_all x1, starting transfers between devices, on_device(): lax.all_to_all(cot_share, MEMBER, split_axis=1, concat_axis=0, tiled=True)  4.35 us
  transfers between devices with their start and end apart: 6, of which 4 were waited for; matrix products, arithmetic and copies ran while one was open for 5% of the time, Pallas kernels for 0%

commit v1 on v0

--- a/solution.py
+++ b/solution.py
@@ -6,6 +6,18 @@
 
 GRID_ROWS = 2048
 MEMBER = ("group", "core")
+
+
+def perform_ladders(mat):
+    return jnp.concatenate(
+        lax.all_to_all(
+            jnp.stack(jnp.split(mat, lax.axis_size(MEMBER), 0)),
+            axis_name=MEMBER,
+            split_axis=0,
+            concat_axis=0,
+        ),
+        1,
+    )
 
 
 def extended(x, sides, width):
@@ -152,9 +164,7 @@
     row_factor = (jnp.cos(latitude) / (band_rows * col_count))[None, None, :, None]
     var_share = var_count // (lax.axis_size("group") * lax.axis_size("core"))
     var_start = lax.axis_index(MEMBER) * var_share
-    collected_members = lax.all_to_all(
-        sample_prediction, MEMBER, split_axis=0, concat_axis=1, tiled=True
-    )
+    collected_members = perform_ladders(sample_prediction)
     sample_group_predictions = collected_members.astype(jnp.float32)
     member_count = sample_group_predictions.shape[1]
     truth = jnp.transpose(

time: 116 us -> 121 us (1.043)
  local copies, waits for them, and re-layouts: 8.12 us -> 11.7 us
    unnamed x17 -> x23, local copies, waits for them, and re-layouts: 1.19 us -> 4.88 us
where the time goes in v1:
time: 121 us; the launch traced here: 120 us
  blocking collectives  46.7 us (39%)
  starting transfers between devices  23.6 us (20%)
  waiting for transfers between devices  17.4 us (14%)
  local copies, waits for them, and re-layouts  11.7 us (10%)
  matrix products  11.4 us (9%)
  other arithmetic  7.28 us (6%)
  between operations  1.76 us (1%)
    all_to_all x1, blocking collectives, all_reduce_sum(): lax.all_to_all(half.reshape(devices, width), peers, 0, 0, tiled=True)  27 us
    all_to_all x1, blocking collectives, all_reduce_sum(): lax.all_to_all(jnp.broadcast_to(own, (devices, width)), peers, 0, 0, tile...  19.7 us
    all_to_all x1, starting transfers between devices, perform_ladders(): lax.all_to_all(jnp.stack(jnp.split(mat, lax.axis_size(MEMBER), 0)), axis_...  8.75 us
    all_to_all x1, waiting for transfers between devices, on_device(): lax.all_to_all(cot_share, MEMBER, split_axis=1, concat_axis=0, tiled=True)  8.71 us
    all_to_all x1, waiting for transfers between devices, perform_ladders(): lax.all_to_all(jnp.stack(jnp.split(mat, lax.axis_size(MEMBER), 0)), axis_...  6.9 us
    dot_general x6, matrix products, feature_conv(): jnp.einsum('mrwc,cd->mrwd', shifted[:, i:i + out_rows], kernel[i].reshape...  5.26 us
    unnamed x23, local copies, waits for them, and re-layouts  4.88 us
    ppermute x1, starting transfers between devices, extended(): lax.ppermute(x, axis, up)  4.49 us
  transfers between devices with their start and end apart: 6, of which 4 were waited for; matrix products, arithmetic and copies ran while one was open for 5% of the time, Pallas kernels for 0%

profile of v1, /device:TPU:1, one launch (start us, length us, event | category | flops | bytes accessed | tf_op | source)
XLA Modules:
  0.0 119.8 jit_solution(1149089941668372214)
XLA Ops:
  0.7 4.5 %collective-permute-start = (bf16[4,32,256]{2,1,0:T(8,128)(2,1)}, bf16[4,32,256]{2,1,0:T(8,128)(2,1)S(1)}, u32[]{:S(2)}, u32[]{:S(2)}) collective-permute-start(bf16[4,32,256]{2,1,0:T(8,128)(2,1)} %param.11), channel_id=1, source_target_pairs={{0,1},{1,2},{2,3},{3,4},{4,5},{5,6},{6,7},{7,8},{8,9},{9,10},{10,1... | collective-permute-start | bytes 196616 | tf_op jit(solution)/shard_map/ppermute | solution.py:28
  5.2 1.3 %collective-permute-start.1 = (bf16[4,32,256]{2,1,0:T(8,128)(2,1)}, bf16[4,32,256]{2,1,0:T(8,128)(2,1)S(1)}, u32[]{:S(2)}, u32[]{:S(2)}) collective-permute-start(bf16[4,32,256]{2,1,0:T(8,128)(2,1)} %param.11), channel_id=1, source_target_pairs={{1,0},{2,1},{3,2},{4,3},{5,4},{6,5},{7,6},{8,7},{9,8},{10,9},{11,1... | collective-permute-start | bytes 196616 | tf_op jit(solution)/shard_map/ppermute | solution.py:29
  6.5 0.9 convert_bitcast_fusion
  7.3 0.9 fusion.59
  8.2 0.8 fusion.75
  9.1 1.0 fusion.73
  10.2 1.0 fusion.72
  12.0 0.5 fusion.74
  13.1 0.9 fusion.23
  14.0 0.6 pad_slice_fusion.1
  14.6 0.8 fusion.70
  15.4 0.8 fusion.71
  16.2 1.2 fusion.22
  17.4 0.4 pad_slice_fusion.9
  17.8 0.6 fusion.69
  18.4 0.6 convolution_add_fusion.1
  19.0 1.4 %fusion.29 = (f32[2,4,256,128]{3,2,1,0:T(8,128)S(1)}, bf16[2,4,256,128]{3,2,1,0:T(8,128)(2,1)S(1)}) fusion(bf16[2,8,256,128]{3,2,1,0:T(8,128)(2,1)S(1)} %fusion.23, f32[2,4,256,128]{3,2,1,0:T(8,128)S(1)} %convolution_add_fusion.1, bf16[384,128,1,1]{1,0,3,2:T(8,128)(2,1)S(1)} %bitcast.217, bf16[2,6,256,128]{3,2,1,0:T(8,128)(2,1)S(1)} %get-tuple-element.15, ...), kind=kOutput, calls=%fused_computation.51 | convolution fusion | flops 214171648 | bytes 5603328 | tf_op jit(solution)/shard_map/mrwc,cd->mrwd/dot_general | solution.py:56
  20.7 0.6 constant_dynamic-update-slice_fusion.7
  21.3 0.6 constant_dynamic-update-slice_fusion.6
  21.9 0.6 constant_dynamic-update-slice_fusion.5
  22.5 0.6 constant_dynamic-update-slice_fusion.4
  23.2 0.6 constant_dynamic-update-slice_fusion.3
  23.8 0.6 constant_dynamic-update-slice_fusion.2
  24.4 0.6 constant_dynamic-update-slice_fusion.1
  25.0 0.6 constant_dynamic-update-slice_fusion
  25.6 8.8 %all-to-all-start = ((bf16[8,4,2,4,256]{4,1,3,2,0:T(4,128)(2,1)}), bf16[8,4,2,4,256]{4,1,3,2,0:T(4,128)(2,1)S(1)}, u32[]{:S(2)}, u32[]{:S(2)}) async-start(bf16[8,4,2,4,256]{4,1,3,2,0:T(4,128)(2,1)} %constant_dynamic-update-slice_fusion), calls=%async_computation | async-start | bytes 262144 | tf_op jit(solution)/shard_map/all_to_all | solution.py:13
  34.4 0.7 convert_bitcast_fusion.1
  35.8 6.9 %all-to-all-done = bf16[8,4,2,4,256]{4,1,3,2,0:T(4,128)(2,1)S(1)} async-done(((bf16[8,4,2,4,256]{4,1,3,2,0:T(4,128)(2,1)}), bf16[8,4,2,4,256]{4,1,3,2,0:T(4,128)(2,1)S(1)}, u32[]{:S(2)}, u32[]{:S(2)}) %all-to-all-start) | async-done | bytes 131104 | tf_op jit(solution)/shard_map/all_to_all | solution.py:13
  43.0 2.3 %fusion.1 = (f32[4,16,4,256]{3,2,1,0:T(4,128)S(1)}, f32[4,4,256]{2,1,0:T(4,128)S(1)}) fusion(f32[4,16,4,256]{3,1,2,0:T(8,128)S(1)} %copy.132, f32[4,16,4,256]{3,2,1,0:T(4,128)S(1)} %copy.90), kind=kLoop, calls=%fused_computation.3 | loop fusion | flops 5173248 | bytes 802816 | tf_op jit(solution)/shard_map/reduce_sum | solution.py:175
  45.5 0.7 copy.94
  46.2 4.3 %all-to-all-start.1 = ((bf16[4,16,4,256]{3,2,0,1:T(4,128)(2,1)}), bf16[4,16,4,256]{3,2,0,1:T(4,128)(2,1)S(1)}, u32[]{:S(2)}, u32[]{:S(2)}) async-start(bf16[4,16,4,256]{3,2,0,1:T(4,128)(2,1)} %copy.94), calls=%async_computation.1 | async-start | bytes 262144 | tf_op jit(solution)/shard_map/all_to_all | solution.py:187
  50.6 8.7 %all-to-all-done.1 = bf16[4,16,4,256]{3,2,0,1:T(4,128)(2,1)S(1)} async-done(((bf16[4,16,4,256]{3,2,0,1:T(4,128)(2,1)}), bf16[4,16,4,256]{3,2,0,1:T(4,128)(2,1)S(1)}, u32[]{:S(2)}, u32[]{:S(2)}) %all-to-all-start.1) | async-done | bytes 131104 | tf_op jit(solution)/shard_map/all_to_all | solution.py:187
  59.6 0.4 fusion.18
  59.9 0.3 convolution_bitcast_fusion.7
  60.6 0.3 convolution_bitcast_fusion.6
  61.0 0.3 convolution_bitcast_fusion.9
  61.7 0.3 convolution_bitcast_fusion.8
  62.7 0.3 convolution_bitcast_fusion.4
  63.4 1.3 %collective-permute-start.2 = (f32[81920]{0:T(1024)S(1)}, f32[81920]{0:T(1024)S(1)}, u32[]{:S(2)}, u32[]{:S(2)}) collective-permute-start(f32[81920]{0:T(1024)S(1)} %slice_select_fusion), channel_id=1, source_target_pairs={{0,32},{32,0},{1,33},{33,1},{2,34},{34,2},{3,35},{35,3},{4,36},{36... | collective-permute-start | bytes 983048 | tf_op jit(solution)/shard_map/ppermute | solution.py:101
  64.7 1.3 %collective-permute-done.2 = f32[81920]{0:T(1024)S(1)} collective-permute-done((f32[81920]{0:T(1024)S(1)}, f32[81920]{0:T(1024)S(1)}, u32[]{:S(2)}, u32[]{:S(2)}) %collective-permute-start.2) | collective-permute-done | bytes 327712 | tf_op jit(solution)/shard_map/ppermute | solution.py:101
  66.1 27.0 %all_to_all.38 = f32[128,1,640]{2,1,0:T(1,128)S(1)} all-to-all(f32[128,1,640]{2,1,0:T(1,128)S(1)} %bitcast.212), channel_id=1, replica_groups=mesh['group'=4,'core'=2,'tile'=32] {'group','tile'}, dimensions={0} | all-to-all | bytes 655360 | tf_op jit(solution)/shard_map/all_to_all | solution.py:102
  93.4 19.7 %all_to_all.39 = f32[128,1,640]{2,1,0:T(1,128)S(1)} all-to-all(f32[128,1,640]{2,1,0:T(1,128)S(1)} %broadcast_in_dim.29), channel_id=1, replica_groups=mesh['group'=4,'core'=2,'tile'=32] {'group','tile'}, dimensions={0} | all-to-all | bytes 655360 | tf_op jit(solution)/shard_map/all_to_all | solution.py:104
  113.2 3.4 %collective-permute-start.3 = (f32[81920]{0:T(1024)S(1)}, f32[81920]{0:T(1024)S(1)}, u32[]{:S(2)}, u32[]{:S(2)}) collective-permute-start(f32[81920]{0:T(1024)S(1)} %bitcast.208), channel_id=1, source_target_pairs={{0,32},{32,0},{1,33},{33,1},{2,34},{34,2},{3,35},{35,3},{4,36},{36... | collective-permute-start | bytes 983048 | tf_op jit(solution)/shard_map/ppermute | solution.py:106
  116.7 0.6 fusion.56
  117.3 0.5 collective-permute-done.3
  117.9 0.9 slice.204
  118.7 0.5 slice.205
  119.2 0.6 fusion.54
  (56 shorter events, 4.8 us)
Async XLA Ops:
  0.6 11.4 %copy-start = (bf16[3,3,32,128]{3,2,1,0:T(8,128)(2,1)S(1)}, bf16[3,3,32,128]{3,2,1,0:T(8,128)(2,1)}, u32[]{:S(2)}) copy-start(bf16[3,3,32,128]{3,2,1,0:T(8,128)(2,1)} %param.17) | copy-start | bytes 221188
  0.6 10.6 %copy-start.1 = (bf16[4,32,256]{2,1,0:T(8,128)(2,1)S(1)}, bf16[4,32,256]{2,1,0:T(8,128)(2,1)}, u32[]{:S(2)}) copy-start(bf16[4,32,256]{2,1,0:T(8,128)(2,1)} %param.11) | copy-start | bytes 196612
  0.7 10.6 %collective-permute-start = (bf16[4,32,256]{2,1,0:T(8,128)(2,1)}, bf16[4,32,256]{2,1,0:T(8,128)(2,1)S(1)}, u32[]{:S(2)}, u32[]{:S(2)}) collective-permute-start(bf16[4,32,256]{2,1,0:T(8,128)(2,1)} %param.11), channel_id=1, source_target_pairs={{0,1},{1,2},{2,3},{3,4},{4,5},{5,6},{6,7},{7,8},{8,9},{9,10},{10,1... | collective-permute-start | bytes 196616 | tf_op jit(solution)/shard_map/ppermute | solution.py:28
  5.2 6.1 %collective-permute-start.1 = (bf16[4,32,256]{2,1,0:T(8,128)(2,1)}, bf16[4,32,256]{2,1,0:T(8,128)(2,1)S(1)}, u32[]{:S(2)}, u32[]{:S(2)}) collective-permute-start(bf16[4,32,256]{2,1,0:T(8,128)(2,1)} %param.11), channel_id=1, source_target_pairs={{1,0},{2,1},{3,2},{4,3},{5,4},{6,5},{7,6},{8,7},{9,8},{10,9},{11,1... | collective-permute-start | bytes 196616 | tf_op jit(solution)/shard_map/ppermute | solution.py:29
  19.0 1.4 %copy-start.2 = (bf16[128,32]{0,1:T(8,128)(2,1)S(1)}, bf16[128,32]{0,1:T(8,128)(2,1)}, u32[]{:S(2)}) copy-start(bf16[128,32]{0,1:T(8,128)(2,1)} %param.20) | copy-start | bytes 24580
  19.0 1.4 %copy-start.3 = (f32[32]{0:T(128)S(1)}, f32[32]{0:T(128)}, u32[]{:S(2)}) copy-start(f32[32]{0:T(128)} %param.21) | copy-start | bytes 388
  25.6 17.1 %all-to-all-start = ((bf16[8,4,2,4,256]{4,1,3,2,0:T(4,128)(2,1)}), bf16[8,4,2,4,256]{4,1,3,2,0:T(4,128)(2,1)S(1)}, u32[]{:S(2)}, u32[]{:S(2)}) async-start(bf16[8,4,2,4,256]{4,1,3,2,0:T(4,128)(2,1)} %constant_dynamic-update-slice_fusion), calls=%async_computation | async-start | bytes 262144 | tf_op jit(solution)/shard_map/all_to_all | solution.py:13
  46.2 13.1 %all-to-all-start.1 = ((bf16[4,16,4,256]{3,2,0,1:T(4,128)(2,1)}), bf16[4,16,4,256]{3,2,0,1:T(4,128)(2,1)S(1)}, u32[]{:S(2)}, u32[]{:S(2)}) async-start(bf16[4,16,4,256]{3,2,0,1:T(4,128)(2,1)} %copy.94), calls=%async_computation.1 | async-start | bytes 262144 | tf_op jit(solution)/shard_map/all_to_all | solution.py:187
  63.4 2.6 %collective-permute-start.2 = (f32[81920]{0:T(1024)S(1)}, f32[81920]{0:T(1024)S(1)}, u32[]{:S(2)}, u32[]{:S(2)}) collective-permute-start(f32[81920]{0:T(1024)S(1)} %slice_select_fusion), channel_id=1, source_target_pairs={{0,32},{32,0},{1,33},{33,1},{2,34},{34,2},{3,35},{35,3},{4,36},{36... | collective-permute-start | bytes 983048 | tf_op jit(solution)/shard_map/ppermute | solution.py:101
  113.2 4.6 %collective-permute-start.3 = (f32[81920]{0:T(1024)S(1)}, f32[81920]{0:T(1024)S(1)}, u32[]{:S(2)}, u32[]{:S(2)}) collective-permute-start(f32[81920]{0:T(1024)S(1)} %bitcast.208), channel_id=1, source_target_pairs={{0,32},{32,0},{1,33},{33,1},{2,34},{34,2},{3,35},{35,3},{4,36},{36... | collective-permute-start | bytes 983048 | tf_op jit(solution)/shard_map/ppermute | solution.py:106
